TPU v7x, 128 devices: a whole 4x4x4 slice. The times are simulated.
128 devices in a mesh: row: 16 (over z_lo, x, core), col: 8 (over y, z_hi).
Axes of the slice: x: 4, y: 4, z: 4 (z_hi: 2, z_lo: 2; z = z_hi * 2 + z_lo), core: 2. Of those that a mesh axis runs over, the one named last changes fastest.
Arguments:
- shared_rows: float32 [2048, 16384], P('row', 'col'), may hold values from -0.125 to 0.125
- event_counts: int32 [16], replicated, may hold values from 32 to 128, as said below
- ridge: float32 [16384], P('col'), may hold values from 0.5 to 2
- items: float32 [1024, 16384], P('row', 'col'), may hold values from -6 to 6
- cand_ids: int32 [512], replicated, may hold values from 0 to 1023
- theta: float32 [16384], P('col'), may hold values from -0.046875 to 0.046875
Outputs:
- gram_tile: float32 [16384, 16384], P('row', 'col')
- scores: float32 [512], replicated
Inputs may be any that keep to these rules, and one draw needn't show every extreme that they name: event_counts[s] counts the live slots at the start of row shard s's 128 slots; some shard is full.
All inputs are finite; a program needn't handle non-finite values.
Results may differ from a plain program's by a relative error of at most 0.000068.
Values sent between devices are 32-bit elements; how exact they have to be, the bound alone decides.
No kernel may reach another device: no remote copies, remote signals or barrier semaphores. Data moves between devices by JAX's collectives and lax.ppermute only.
A program may use at most 128 MiB of HBM per device.

v0:
```python
import jax
import jax.numpy as jnp
from jax import lax
from jax.sharding import PartitionSpec as P

F = 16384
high = lax.Precision.HIGHEST


def spread(value, axis, source):
    kept = jnp.where(lax.axis_index(axis) == source, value, 0).astype(value.dtype)
    return lax.psum(kept, axis)


def body(shared_rows, event_counts, ridge, items, cand_ids, theta):
    ratio = lax.axis_size("row") // lax.axis_size("col")
    row_pos = lax.axis_index("row")
    col_pos = lax.axis_index("col")
    width_col = shared_rows.shape[1]
    width_row = width_col // ratio
    ev_slots = shared_rows.shape[0]
    slot = lax.iota(jnp.int32, ev_slots)
    masked = jnp.where((slot < event_counts[row_pos])[:, None], shared_rows, jnp.float32(0.0))
    offset = row_pos % ratio * width_row
    root = row_pos // ratio
    contract = (((0,), (0,)), ((), ()))
    col_all = lax.all_gather(masked, "row", axis=0, tiled=True)
    row_all = spread(lax.dynamic_slice_in_dim(col_all, offset, width_row, 1), "col", root)
    tile = lax.dot_general(
        row_all, col_all, contract, precision=high, preferred_element_type=jnp.float32
    )
    rows_global = row_pos * width_row + lax.broadcasted_iota(jnp.int32, (width_row, width_col), 0)
    cols_global = col_pos * width_col + lax.broadcasted_iota(jnp.int32, (width_row, width_col), 1)
    tile = tile + jnp.where(rows_global == cols_global, ridge[None, :], jnp.float32(0.0))
    items_dev = items.shape[0]
    onehot = (
        cand_ids[:, None] == row_pos * items_dev + lax.iota(jnp.int32, items_dev)[None, :]
    ).astype(jnp.float32)
    picked = jnp.dot(onehot, items, precision=high, preferred_element_type=jnp.float32)
    cand_col = lax.psum(picked, "row")
    across = (((1,), (1,)), ((), ()))
    cand_row = spread(lax.dynamic_slice_in_dim(cand_col, offset, width_row, 1), "col", root)
    image_part = lax.dot_general(
        cand_col, tile, across, precision=high, preferred_element_type=jnp.float32
    )
    image_row = lax.psum(image_part, "col")
    quad = jnp.where(col_pos == 0, jnp.sum(cand_row * image_row, axis=1), jnp.float32(0.0))
    linear = jnp.where(
        row_pos == 0,
        jnp.dot(cand_col, theta, precision=high, preferred_element_type=jnp.float32),
        jnp.float32(0.0),
    )
    quad_all, linear_all = lax.psum((quad, linear), ("row", "col"))
    return (tile, linear_all + jnp.sqrt(quad_all / F))


def solution(mesh):
    return jax.shard_map(
        body,
        mesh=mesh,
        in_specs=(P("row", "col"), P(), P("col"), P("row", "col"), P(), P("col")),
        out_specs=(P("row", "col"), P()),
        check_vma=False,
    )
```

profile of v0, /device:TPU:1, one launch (start us, length us, event | category | flops | bytes accessed | tf_op | source)
XLA Modules:
  0.0 940.3 jit_solution(5957106584917055528)
XLA Ops:
  7.2 0.0 copy-start
  7.2 0.0 all-gather.2.cloned.1.call-start
  7.2 1.3 dynamic_slice.9
  8.5 0.6 iota_compare_fusion
  9.2 2.3 broadcast_select_fusion
  11.5 0.0 all-gather.2.cloned.1.call-update
  11.5 0.0 all-reduce.8.cloned.1.call-start
  11.6 0.0 copy-done
  11.6 4.5 fusion
  16.1 0.0 all-reduce.8.cloned.1.call-update
  16.1 0.0 all-reduce.6.cloned.1.call-start
  16.2 90.8 %all-gather.2.cloned.1.call-done = f32[2048,2048]{1,0:T(8,128)} async-done(((f32[128,2048]{1,0:T(8,128)}), f32[2048,2048]{1,0:T(8,128)}) %all-gather.2.cloned.1.call-update) | async-done | bytes 16777232 | tf_op jit(solution)/shard_map/all_gather | solution.py:27
  107.0 8.7 dynamic-slice_select_fusion
  115.7 0.0 copy-start.3
  115.7 0.0 all-reduce.6.cloned.1.call-update
  115.7 0.0 all-reduce.10.cloned.1.call-start
  115.8 122.9 %all-reduce.8.cloned.1.call-done = f32[512,2048]{1,0:T(8,128)} async-done(((f32[512,2048]{1,0:T(8,128)}), f32[512,2048]{1,0:T(8,128)}) %all-reduce.8.cloned.1.call-update) | async-done | bytes 4194320 | tf_op jit(solution)/shard_map/psum | solution.py:40
  238.7 3.2 dynamic-slice_select_fusion.1
  241.9 343.4 %all-reduce.6.cloned.1.call-done = f32[2048,1024]{1,0:T(8,128)} async-done(((f32[2048,1024]{1,0:T(8,128)}), f32[2048,1024]{1,0:T(8,128)}) %all-reduce.6.cloned.1.call-update) | async-done | bytes 8388624 | tf_op jit(solution)/shard_map/psum | solution.py:12
  585.3 0.0 copy-done.3
  585.3 67.7 %select_add_fusion = f32[1024,2048]{1,0:T(8,128)S(1)} fusion(f32[2048]{0:T(1024)S(1)} %copy-done.3, s32[2048]{0:T(1024)S(1)} %iota_add_fusion, s32[1024]{0:T(1024)S(1)} %iota_add_fusion.1, f32[2048,1024]{1,0:T(8,128)} %all-reduce.6.cloned.1.call-done, f32[2048,2048]{1,0:T(8,128)} %all-gather.2.cloned.1.call-done), kind=kOutput, calls=%fused_computation | convolution fusion | flops 51545899008 | bytes 33574912 | tf_op jit(solution)/shard_map/dot_general | solution.py:29
  653.1 0.0 copy-start.4
  653.1 3.4 copy-done.4
  656.5 0.0 copy-done.1
  656.5 15.2 %fusion.5 = f32[512,1024]{1,0:T(8,128)} fusion(f32[512,2048]{1,0:T(8,128)S(1)} %copy-done.1, f32[1024,2048]{1,0:T(8,128)S(1)} %select_add_fusion), kind=kOutput, calls=%fused_computation.17 | convolution fusion | flops 12884901888 | bytes 14680064 | tf_op jit(solution)/shard_map/dot_general | solution.py:43
  671.7 0.0 all-reduce.10.cloned.1.call-update
  671.7 0.0 copy-done.2
  671.7 5.8 fusion.4
  677.5 185.2 %all-reduce.10.cloned.1.call-done = (f32[512,1024]{1,0:T(8,128)}, f32[512,1024]{1,0:T(8,128)}) async-done(((f32[512,1024]{1,0:T(8,128)}, f32[512,1024]{1,0:T(8,128)}), (f32[512,1024]{1,0:T(8,128)}, f32[512,1024]{1,0:T(8,128)})) %all-reduce.10.cloned.1.call-update) | async-done | bytes 4194320 | tf_op jit(solution)/shard_map/psum | solution.py:12
  862.7 2.5 multiply_reduce_fusion
  865.2 67.8 %all-reduce = (f32[512]{0:T(512)S(1)}, f32[512]{0:T(512)S(1)}) all-reduce(f32[512]{0:T(512)S(1)} %broadcast_select_fusion.2, f32[512]{0:T(512)S(1)} %broadcast_select_fusion.1), channel_id=1, replica_groups=mesh['row'=16,'col'=8] {'row','col'}, use_global_device_ids=true, to_apply=%region_2.3 | all-reduce | flops 1024 | bytes 8192 | tf_op jit(solution)/shard_map/psum | solution.py:53
  933.0 0.6 sqrt_add_fusion
  (7 shorter events, 0.0 us)
Async XLA Ops:
  7.2 4.4 copy-start
  7.2 99.8 %all-gather.2.cloned.1.call-start = ((), (), s32[]{:S(2)}) async-start(), calls=%async_computation | async-start | bytes 17825792 | tf_op jit(solution)/shard_map/all_gather | solution.py:27
  11.5 227.2 %all-reduce.8.cloned.1.call-start = ((), (), s32[]{:S(2)}) async-start(), calls=%async_computation.2 | async-start | bytes 8388608 | tf_op jit(solution)/shard_map/psum | solution.py:40
  16.1 569.2 %all-reduce.6.cloned.1.call-start = ((), (), s32[]{:S(2)}) async-start(), calls=%async_computation.1 | async-start | bytes 16777216 | tf_op jit(solution)/shard_map/psum | solution.py:12
  115.7 469.7 %copy-start.3 = (f32[2048]{0:T(1024)S(1)}, f32[2048]{0:T(1024)}, u32[]{:S(2)}) copy-start(f32[2048]{0:T(1024)} %param.8) | copy-start | bytes 24580
  115.7 747.0 %all-reduce.10.cloned.1.call-start = ((), (), s32[]{:S(2)}) async-start(), calls=%async_computation.3 | async-start | bytes 8388608 | tf_op jit(solution)/shard_map/psum | solution.py:12
  585.3 71.1 %copy-start.1 = (f32[512,2048]{1,0:T(8,128)S(1)}, f32[512,2048]{1,0:T(8,128)}, u32[]{:S(2)}) copy-start(f32[512,2048]{1,0:T(8,128)} %all-reduce.8.cloned.1.call-done) | copy-start | bytes 12582916
  653.1 3.4 copy-start.4
  656.5 15.3 %copy-start.2 = (f32[2048]{0:T(1024)S(1)}, f32[2048]{0:T(1024)}, u32[]{:S(2)}) copy-start(f32[2048]{0:T(1024)} %param.11) | copy-start | bytes 24580
Sparse Core Ops, SparseCore 0:
  11.7 95.2 all-gather.1
  109.5 129.1 all-reduce.7
  241.8 343.4 all-reduce.5
  671.8 190.8 all-reduce.9
where the time goes:
time: 944 us; the launch traced here: 940 us
  waiting for transfers between devices  742 us (79%)
  matrix products  93.2 us (10%)
  blocking collectives  67.8 us (7%)
  other arithmetic  18 us (2%)
  between operations  14.1 us (1%)
    psum x2, waiting for transfers between devices, spread(): return lax.psum(kept, axis)  529 us
    psum x1, waiting for transfers between devices, body(): cand_col = lax.psum(picked, 'row')  123 us
    all_gather x1, waiting for transfers between devices, body(): col_all = lax.all_gather(masked, 'row', axis=0, tiled=True)  90.8 us
    psum x1, blocking collectives, body(): quad_all, linear_all = lax.psum((quad, linear), ('row', 'col'))  67.8 us
    dot_general x1, matrix products, body(): lax.dot_general(row_all, col_all, contract, precision=high, preferred_ele...  67.7 us
  transfers between devices with their start and end apart: 4, of which 4 were waited for; matrix products, arithmetic and copies ran while one was open for 2% of the time, Pallas kernels for 0%

commit v1 on v0

--- a/solution.py
+++ b/solution.py
@@ -5,6 +5,11 @@
 
 F = 16384
 high = lax.Precision.HIGHEST
+
+
+def one_after_other(value_2, first, second):
+    half = lax.psum(value_2, first)
+    return lax.psum(half, second)
 
 
 def spread(value, axis, source):
@@ -50,7 +55,7 @@
         jnp.dot(cand_col, theta, precision=high, preferred_element_type=jnp.float32),
         jnp.float32(0.0),
     )
-    quad_all, linear_all = lax.psum((quad, linear), ("row", "col"))
+    quad_all, linear_all = one_after_other((quad, linear), "row", "col")
     return (tile, linear_all + jnp.sqrt(quad_all / F))
 
 

time: 944 us -> 916 us (0.970)
  blocking collectives: 67.8 us -> 46.7 us
    psum x1 -> x2, blocking collectives: 67.8 us -> 46.7 us  [the longest x1 27.2 us: one_after_other(): half = lax.psum(value_2, first)]
where the time goes in v1:
time: 916 us; the launch traced here: 910 us
  waiting for transfers between devices  742 us (81%)
  matrix products  84.4 us (9%)
  blocking collectives  46.7 us (5%)
  other arithmetic  18 us (2%)
  between operations  13.9 us (2%)
    psum x2, waiting for transfers between devices, spread(): return lax.psum(kept, axis)  529 us
    psum x1, waiting for transfers between devices, body(): cand_col = lax.psum(picked, 'row')  123 us
    all_gather x1, waiting for transfers between devices, body(): col_all = lax.all_gather(masked, 'row', axis=0, tiled=True)  90.8 us
    dot_general x1, matrix products, body(): lax.dot_general(row_all, col_all, contract, precision=high, preferred_ele...  58.9 us
    psum x1, blocking collectives, one_after_other(): half = lax.psum(value_2, first)  27.2 us
    psum x1, blocking collectives, one_after_other(): return lax.psum(half, second)  19.5 us
  transfers between devices with their start and end apart: 4, of which 4 were waited for; matrix products, arithmetic and copies ran while one was open for 2% of the time, Pallas kernels for 0%

profile of v1, /device:TPU:1, one launch (start us, length us, event | category | flops | bytes accessed | tf_op | source)
XLA Modules:
  0.0 910.2 jit_solution(13510939555130197497)
XLA Ops:
  7.2 0.0 copy-start
  7.2 0.0 all-gather.2.cloned.1.call-start
  7.2 1.3 dynamic_slice.9
  8.5 0.6 iota_compare_fusion
  9.2 2.3 broadcast_select_fusion
  11.5 0.0 all-gather.2.cloned.1.call-update
  11.5 0.0 all-reduce.9.cloned.1.call-start
  11.6 0.0 copy-done
  11.6 4.5 fusion
  16.1 0.0 all-reduce.9.cloned.1.call-update
  16.1 0.0 all-reduce.7.cloned.1.call-start
  16.2 90.8 %all-gather.2.cloned.1.call-done = f32[2048,2048]{1,0:T(8,128)} async-done(((f32[128,2048]{1,0:T(8,128)}), f32[2048,2048]{1,0:T(8,128)}) %all-gather.2.cloned.1.call-update) | async-done | bytes 16777232 | tf_op jit(solution)/shard_map/all_gather | solution.py:32
  107.0 8.7 dynamic-slice_select_fusion
  115.7 0.0 all-reduce.7.cloned.1.call-update
  115.7 0.0 all-reduce.11.cloned.1.call-start
  115.8 122.9 %all-reduce.9.cloned.1.call-done = f32[512,2048]{1,0:T(8,128)} async-done(((f32[512,2048]{1,0:T(8,128)}), f32[512,2048]{1,0:T(8,128)}) %all-reduce.9.cloned.1.call-update) | async-done | bytes 4194320 | tf_op jit(solution)/shard_map/psum | solution.py:45
  238.7 3.2 dynamic-slice_select_fusion.1
  241.9 343.4 %all-reduce.7.cloned.1.call-done = f32[2048,1024]{1,0:T(8,128)} async-done(((f32[2048,1024]{1,0:T(8,128)}), f32[2048,1024]{1,0:T(8,128)}) %all-reduce.7.cloned.1.call-update) | async-done | bytes 8388624 | tf_op jit(solution)/shard_map/psum | solution.py:17
  585.3 0.0 copy-done.3
  585.3 58.9 %select_add_fusion = f32[1024,2048]{1,0:T(8,128)S(1)} fusion(f32[2048]{0:T(1024)S(1)} %copy-done.3, s32[2048]{0:T(1024)S(1)} %iota_add_fusion, s32[1024]{0:T(1024)S(1)} %iota_add_fusion.1, f32[2048,1024]{1,0:T(8,128)} %all-reduce.7.cloned.1.call-done, f32[2048,2048]{1,0:T(8,128)} %all-gather.2.cloned.1.call-done), kind=kOutput, calls=%fused_computation | convolution fusion | flops 51545899008 | bytes 33574912 | tf_op jit(solution)/shard_map/dot_general | solution.py:34
  644.2 0.0 copy-start.4
  644.2 3.4 copy-done.4
  647.6 0.0 copy-done.1
  647.6 15.3 %fusion.5 = f32[512,1024]{1,0:T(8,128)} fusion(f32[512,2048]{1,0:T(8,128)S(1)} %copy-done.1, f32[1024,2048]{1,0:T(8,128)S(1)} %select_add_fusion), kind=kOutput, calls=%fused_computation.17 | convolution fusion | flops 12884901888 | bytes 14680064 | tf_op jit(solution)/shard_map/dot_general | solution.py:48
  662.9 0.0 all-reduce.11.cloned.1.call-update
  662.9 0.0 copy-done.2
  662.9 5.8 fusion.4
  668.7 185.1 %all-reduce.11.cloned.1.call-done = (f32[512,1024]{1,0:T(8,128)}, f32[512,1024]{1,0:T(8,128)}) async-done(((f32[512,1024]{1,0:T(8,128)}, f32[512,1024]{1,0:T(8,128)}), (f32[512,1024]{1,0:T(8,128)}, f32[512,1024]{1,0:T(8,128)})) %all-reduce.11.cloned.1.call-update) | async-done | bytes 4194320 | tf_op jit(solution)/shard_map/psum | solution.py:17
  853.8 2.5 multiply_reduce_fusion
  856.3 27.2 %all-reduce = (f32[512]{0:T(512)S(1)}, f32[512]{0:T(512)S(1)}) all-reduce(f32[512]{0:T(512)S(1)} %broadcast_select_fusion.2, f32[512]{0:T(512)S(1)} %broadcast_select_fusion.1), channel_id=1, replica_groups=mesh['row'=16,'col'=8] {'row'}, use_global_device_ids=true, to_apply=%region_2.3 | all-reduce | flops 1024 | bytes 8192 | tf_op jit(solution)/shard_map/psum | solution.py:11
  883.5 19.5 %all-reduce.1 = (f32[512]{0:T(512)S(1)}, f32[512]{0:T(512)S(1)}) all-reduce(f32[512]{0:T(512)S(1)} %get-tuple-element.2, f32[512]{0:T(512)S(1)} %get-tuple-element.3), channel_id=1, replica_groups=mesh['row'=16,'col'=8] {'col'}, use_global_device_ids=true, to_apply=%region_3.4 | all-reduce | flops 1024 | bytes 8192 | tf_op jit(solution)/shard_map/psum | solution.py:12
  903.0 0.6 sqrt_add_fusion
  (8 shorter events, 0.0 us)
Async XLA Ops:
  7.2 4.4 copy-start
  7.2 99.8 %all-gather.2.cloned.1.call-start = ((), (), s32[]{:S(2)}) async-start(), calls=%async_computation | async-start | bytes 17825792 | tf_op jit(solution)/shard_map/all_gather | solution.py:32
  11.5 227.2 %all-reduce.9.cloned.1.call-start = ((), (), s32[]{:S(2)}) async-start(), calls=%async_computation.2 | async-start | bytes 8388608 | tf_op jit(solution)/shard_map/psum | solution.py:45
  16.1 569.2 %all-reduce.7.cloned.1.call-start = ((), (), s32[]{:S(2)}) async-start(), calls=%async_computation.1 | async-start | bytes 16777216 | tf_op jit(solution)/shard_map/psum | solution.py:17
  115.7 469.7 %copy-start.3 = (f32[2048]{0:T(1024)S(1)}, f32[2048]{0:T(1024)}, u32[]{:S(2)}) copy-start(f32[2048]{0:T(1024)} %param.8) | copy-start | bytes 24580
  115.7 738.2 %all-reduce.11.cloned.1.call-start = ((), (), s32[]{:S(2)}) async-start(), calls=%async_computation.3 | async-start | bytes 8388608 | tf_op jit(solution)/shard_map/psum | solution.py:17
  585.3 62.3 %copy-start.1 = (f32[512,2048]{1,0:T(8,128)S(1)}, f32[512,2048]{1,0:T(8,128)}, u32[]{:S(2)}) copy-start(f32[512,2048]{1,0:T(8,128)} %all-reduce.9.cloned.1.call-done) | copy-start | bytes 12582916
  644.2 3.4 copy-start.4
  647.6 15.3 %copy-start.2 = (f32[2048]{0:T(1024)S(1)}, f32[2048]{0:T(1024)}, u32[]{:S(2)}) copy-start(f32[2048]{0:T(1024)} %param.11) | copy-start | bytes 24580
Sparse Core Ops, SparseCore 0:
  11.7 95.2 all-gather.1
  109.5 129.1 all-reduce.8
  241.8 343.4 all-reduce.6
  663.0 190.7 all-reduce.10
